TPU v7x, 32 devices: a whole 2x2x4 slice. The times are simulated.
32 devices in a mesh: seq: 4 (over y, core), batch: 8 (over z, x).
Axes of the slice: x: 2, y: 2, z: 4, core: 2. Of those that a mesh axis runs over, the one named last changes fastest.
Arguments:
- inputs: bfloat16 [8, 512, 768], P('batch', 'seq'), may hold values from -6 to 6
- cotangent: bfloat16 [8, 512, 768], P('batch', 'seq'), may hold values from -6 to 6
- weight: bfloat16 [768, 2304], replicated, may hold values from -0.125 to 0.125
Outputs:
- grad_input: bfloat16 [8, 512, 768], P('batch', 'seq')
- grad_weight: float32 [768, 2304], P('seq', 'batch')
All inputs are finite; a program needn't handle non-finite values.
Results may differ from a plain program's by a relative error of at most 0.0026.
Values may be sent and summed in bfloat16 or wider, within the bound.
No kernel may reach another device: no remote copies, remote signals or barrier semaphores. Data moves between devices by JAX's collectives and lax.ppermute only.
A program may use at most 64 MiB of HBM per device.

v0:
```python
import math
import jax
import jax.numpy as jnp
from jax import lax
from jax.sharding import PartitionSpec as P

KW = 3
TAP_SPACING = 64


def extended_2(x, sides, width):
    for axis, dim in sides:
        peers, length = (lax.axis_size(axis), x.shape[dim])
        up = [(i, (i + 1) % peers) for i in range(peers - 1)]
        down = [(j, i) for i, j in up]
        last = lax.slice_in_dim(x, length - width, length, axis=dim)
        first = lax.slice_in_dim(x, 0, width, axis=dim)
        before = lax.ppermute(last, axis, up)
        after = lax.ppermute(first, axis, down)
        x = jnp.concatenate([before, x, after], axis=dim)
    return x


def gelu_factors(values):
    normal_cdf = 0.5 * (1.0 + jax.scipy.special.erf(values / math.sqrt(2.0)))
    density = jnp.exp(-0.5 * values * values) / math.sqrt(2.0 * math.pi)
    return (values * normal_cdf, normal_cdf + values * density)


def body(inputs, cotangent, weight):
    middle_offset = KW // 2
    reach = middle_offset * TAP_SPACING
    length = inputs.shape[1]
    in_width = inputs.shape[2]
    padded_input = extended_2(cotangent, (("seq", 1),), reach)
    extended = padded_input[0]
    values = inputs[0].astype(jnp.float32)
    activation, deriv = gelu_factors(values)
    act = activation.astype(jnp.bfloat16)
    grad_act = jnp.zeros((length, in_width), jnp.float32)
    for tap_index in range(KW):
        window_start = (2 * middle_offset - tap_index) * TAP_SPACING
        window = lax.slice_in_dim(extended, window_start, window_start + length, axis=0)
        grad_act = grad_act + jnp.dot(
            window,
            weight[:, tap_index * in_width : (tap_index + 1) * in_width],
            preferred_element_type=jnp.float32,
        )
    grad_input = (grad_act * deriv).astype(jnp.bfloat16)[None]
    seq_count = lax.axis_size("seq")
    batch_count = lax.axis_size("batch")
    counted = batch_count * inputs.shape[0] * length * seq_count
    factor = 1.0 / math.sqrt(float(counted))
    owned = lax.all_to_all(cotangent, "seq", split_axis=2, concat_axis=1, tiled=True)[0]
    own_rows = owned.shape[1]
    owned_padded = jnp.pad(owned, ((reach, reach), (0, 0)))
    whole_act = lax.all_gather(act[None], "seq", axis=1, tiled=True)[0]
    count = whole_act.shape[0]
    updated = []
    for tap_index in range(KW):
        offset = 0 + (2 * middle_offset - tap_index) * TAP_SPACING
        window = lax.dynamic_slice_in_dim(owned_padded, offset, count, 0)
        updated.append(
            lax.dot_general(
                window, whole_act, (((0,), (0,)), ((), ())), preferred_element_type=jnp.float32
            )
        )
    taps_sum = jnp.stack(updated, axis=0)
    local_rows = jnp.transpose(taps_sum, (1, 0, 2)).reshape(own_rows, KW * in_width) * factor
    pieces = local_rows.reshape(own_rows, batch_count, -1)
    swapped = lax.all_to_all(pieces, "batch", split_axis=1, concat_axis=1, tiled=True)
    grad_weight = jnp.sum(swapped, axis=1)
    return (grad_input, grad_weight)


def solution(mesh):
    placed = (P("batch", "seq", None), P("batch", "seq", None), P())
    return jax.shard_map(
        body,
        mesh=mesh,
        in_specs=placed,
        out_specs=(P("batch", "seq", None), P("seq", "batch")),
        check_vma=False,
    )
```

profile of v0, /device:TPU:0, one launch (start us, length us, event | category | flops | bytes accessed | tf_op | source)
XLA Modules:
  0.0 85.2 jit_solution(1251447381360411007)
XLA Ops:
  0.6 0.0 copy-start.1
  0.6 1.3 %copy.8 = bf16[1,128,768]{1,0,2:T(2,128)(2,1)S(1)} copy(bf16[1,128,768]{2,1,0:T(8,128)(2,1)} %param.4) | data formatting | bytes 393216 | tf_op args[1]
  2.0 0.5 broadcast.12
  2.5 1.8 %reduce = bf16[768,128]{1,0:T(8,128)(2,1)S(1)} reduce(bf16[768,1,128]{2,1,0:T(2,128)(2,1)S(1)} %bitcast.78, bf16[]{:T(256)} %broadcast.12), dimensions={1}, to_apply=%bitcast.69.reduce_sub_computation | reduce | bytes 393218
  4.3 0.7 reshape.16
  5.0 4.2 %all-to-all-start = ((bf16[4,2,12288]{2,1,0:T(2,128)(2,1)}), bf16[4,2,12288]{2,1,0:T(2,128)(2,1)S(1)}, u32[]{:S(2)}, u32[]{:S(2)}) async-start(bf16[4,2,12288]{2,1,0:T(2,128)(2,1)} %reshape.16), calls=%async_computation | async-start | bytes 393216 | tf_op jit(solution)/shard_map/all_to_all | solution.py:54
  9.2 0.0 copy-done.1
  9.2 0.1 fusion.30
  9.3 10.3 %all_gather.3 = bf16[1,512,768]{2,1,0:T(8,128)(2,1)S(1)} all-gather(bf16[1,128,768]{2,1,0:T(8,128)(2,1)S(1)} %fusion.30), channel_id=1, replica_groups=mesh['seq'=4,'batch'=8] {'seq'}, dimensions={1}, use_global_device_ids=true | all-gather | bytes 983040 | tf_op jit(solution)/shard_map/all_gather | solution.py:57
  19.7 0.0 all-to-all-done
  19.7 0.2 reshape.17
  19.9 0.2 copy.9
  20.1 0.4 convolution_bitcast_fusion.1
  20.5 0.4 convolution_bitcast_fusion.2
  20.8 0.3 convolution_bitcast_fusion
  21.2 0.1 fusion
  21.3 1.9 %copy.10 = f32[192,3,768]{0,2,1:T(8,128)} copy(f32[192,3,768]{2,0,1:T(8,128)S(1)} %fusion) | data formatting | bytes 3538944 | tf_op jit(solution)/shard_map/mul | solution.py:69
  23.3 0.0 copy-start
  23.3 6.5 %all-to-all-start.1 = ((f32[192,8,288]{0,2,1:T(8,128)}), f32[192,8,288]{0,2,1:T(8,128)S(1)}, u32[]{:S(2)}, u32[]{:S(2)}) async-start(f32[192,8,288]{0,2,1:T(8,128)} %bitcast.72), calls=%async_computation.1 | async-start | bytes 4718592 | tf_op jit(solution)/shard_map/all_to_all | solution.py:71
  29.7 0.0 copy-done
  29.8 2.0 %collective-permute-start.1 = (bf16[1,64,768]{2,1,0:T(8,128)(2,1)S(1)}, bf16[1,64,768]{2,1,0:T(8,128)(2,1)S(1)}, u32[]{:S(2)}, u32[]{:S(2)}) collective-permute-start(bf16[1,64,768]{2,1,0:T(8,128)(2,1)S(1)} %get-tuple-element.5), channel_id=1, source_target_pairs={{0,8},{8,16},{16,24},{1,9},{9,17},{17,25},{2,10},{10,18},{18,26},{... | collective-permute-start | bytes 294920 | tf_op jit(solution)/shard_map/ppermute | solution.py:18
  31.8 1.3 %collective-permute-start = (bf16[1,64,768]{2,1,0:T(8,128)(2,1)S(1)}, bf16[1,64,768]{2,1,0:T(8,128)(2,1)S(1)}, u32[]{:S(2)}, u32[]{:S(2)}) collective-permute-start(bf16[1,64,768]{2,1,0:T(8,128)(2,1)S(1)} %get-tuple-element.4), channel_id=1, source_target_pairs={{8,0},{16,8},{24,16},{9,1},{17,9},{25,17},{10,2},{18,10},{26,18},{... | collective-permute-start | bytes 294920 | tf_op jit(solution)/shard_map/ppermute | solution.py:19
  33.1 1.6 %fusion.5 = f32[128,768]{1,0:T(8,128)S(1)} fusion(bf16[768,2304]{1,0:T(8,128)(2,1)} %param.5, bf16[1,128,768]{2,1,0:T(8,128)(2,1)S(1)} %copy-done), kind=kOutput, calls=%fused_computation.10 | convolution fusion | flops 150994944 | bytes 1769472 | tf_op jit(solution)/shard_map/dot_general | solution.py:44
  34.7 0.0 collective-permute-done.1
  34.7 1.6 %fusion.3 = f32[128,768]{1,0:T(8,128)S(1)} fusion(bf16[768,2304]{1,0:T(8,128)(2,1)} %param.5, bf16[1,128,768]{2,1,0:T(8,128)(2,1)S(1)} %copy-done, bf16[1,64,768]{2,1,0:T(8,128)(2,1)S(1)} %collective-permute-done.1), kind=kOutput, calls=%fused_computation.8 | convolution fusion | flops 151388160 | bytes 1867776 | tf_op jit(solution)/shard_map/dot_general | solution.py:44
  36.3 0.0 collective-permute-done
  36.3 2.4 %fusion.11 = bf16[1,128,768]{2,1,0:T(8,128)(2,1)} fusion(f32[128,768]{1,0:T(8,128)S(1)} %fusion.3, f32[128,768]{1,0:T(8,128)S(1)} %fusion.5, bf16[768,2304]{1,0:T(8,128)(2,1)} %param.5, bf16[1,128,768]{2,1,0:T(8,128)(2,1)S(1)} %copy-done.1, bf16[1,64,768]{2,1,0:T(8,128)(2,1)S(1)} %collective-permute-done, bf16[1,128,768]{2,1,0:T(8,128)(2,1)S(1)} %copy-done), kind=kOutput, calls=%fused_computation.14 | convolution fusion | flops 152666112 | bytes 2654208 | tf_op jit(solution)/shard_map/dot_general | solution.py:44
  38.6 45.5 %all-to-all-done.1 = f32[192,8,288]{0,2,1:T(8,128)S(1)} async-done(((f32[192,8,288]{0,2,1:T(8,128)}), f32[192,8,288]{0,2,1:T(8,128)S(1)}, u32[]{:S(2)}, u32[]{:S(2)}) %all-to-all-start.1) | async-done | bytes 1769504 | tf_op jit(solution)/shard_map/all_to_all | solution.py:71
  84.1 0.2 reduce_sum.9
  84.3 0.9 %copy.11 = f32[192,288]{1,0:T(8,128)} copy(f32[192,288]{0,1:T(8,128)S(1)} %reduce_sum.9) | data formatting | bytes 442368
  (3 shorter events, 0.1 us)
Async XLA Ops:
  0.6 8.6 %copy-start.1 = (bf16[1,128,768]{2,1,0:T(8,128)(2,1)S(1)}, bf16[1,128,768]{2,1,0:T(8,128)(2,1)}, u32[]{:S(2)}) copy-start(bf16[1,128,768]{2,1,0:T(8,128)(2,1)} %param.3) | copy-start | bytes 589828
  5.0 14.7 %all-to-all-start = ((bf16[4,2,12288]{2,1,0:T(2,128)(2,1)}), bf16[4,2,12288]{2,1,0:T(2,128)(2,1)S(1)}, u32[]{:S(2)}, u32[]{:S(2)}) async-start(bf16[4,2,12288]{2,1,0:T(2,128)(2,1)} %reshape.16), calls=%async_computation | async-start | bytes 393216 | tf_op jit(solution)/shard_map/all_to_all | solution.py:54
  23.3 6.5 %copy-start = (bf16[1,128,768]{2,1,0:T(8,128)(2,1)S(1)}, bf16[1,128,768]{2,1,0:T(8,128)(2,1)}, u32[]{:S(2)}) copy-start(bf16[1,128,768]{2,1,0:T(8,128)(2,1)} %param.4) | copy-start | bytes 589828
  23.3 60.9 %all-to-all-start.1 = ((f32[192,8,288]{0,2,1:T(8,128)}), f32[192,8,288]{0,2,1:T(8,128)S(1)}, u32[]{:S(2)}, u32[]{:S(2)}) async-start(f32[192,8,288]{0,2,1:T(8,128)} %bitcast.72), calls=%async_computation.1 | async-start | bytes 4718592 | tf_op jit(solution)/shard_map/all_to_all | solution.py:71
  29.8 4.9 %collective-permute-start.1 = (bf16[1,64,768]{2,1,0:T(8,128)(2,1)S(1)}, bf16[1,64,768]{2,1,0:T(8,128)(2,1)S(1)}, u32[]{:S(2)}, u32[]{:S(2)}) collective-permute-start(bf16[1,64,768]{2,1,0:T(8,128)(2,1)S(1)} %get-tuple-element.5), channel_id=1, source_target_pairs={{0,8},{8,16},{16,24},{1,9},{9,17},{17,25},{2,10},{10,18},{18,26},{... | collective-permute-start | bytes 294920 | tf_op jit(solution)/shard_map/ppermute | solution.py:18
  31.8 4.5 %collective-permute-start = (bf16[1,64,768]{2,1,0:T(8,128)(2,1)S(1)}, bf16[1,64,768]{2,1,0:T(8,128)(2,1)S(1)}, u32[]{:S(2)}, u32[]{:S(2)}) collective-permute-start(bf16[1,64,768]{2,1,0:T(8,128)(2,1)S(1)} %get-tuple-element.4), channel_id=1, source_target_pairs={{8,0},{16,8},{24,16},{9,1},{17,9},{25,17},{10,2},{18,10},{26,18},{... | collective-permute-start | bytes 294920 | tf_op jit(solution)/shard_map/ppermute | solution.py:19
where the time goes:
time: 85.6 us; the launch traced here: 85.2 us
  waiting for transfers between devices  45.5 us (53%)
  starting transfers between devices  14 us (16%)
  blocking collectives  10.3 us (12%)
  matrix products  6.62 us (8%)
  local copies, waits for them, and re-layouts  5.77 us (7%)
  other arithmetic  2.18 us (3%)
    all_to_all x1, waiting for transfers between devices, body(): lax.all_to_all(pieces, 'batch', split_axis=1, concat_axis=1, tiled=True)  45.5 us
    all_gather x1, blocking collectives, body(): whole_act = lax.all_gather(act[None], 'seq', axis=1, tiled=True)[0]  10.3 us
    all_to_all x1, starting transfers between devices, body(): lax.all_to_all(pieces, 'batch', split_axis=1, concat_axis=1, tiled=True)  6.48 us
    dot_general x3, matrix products, body(): jnp.dot(window, weight[:, tap_index * in_width:(tap_index + 1) * in_width...  5.54 us
    all_to_all x1, starting transfers between devices, body(): lax.all_to_all(cotangent, 'seq', split_axis=2, concat_axis=1, tiled=True)[0]  4.24 us
    unnamed x11, local copies, waits for them, and re-layouts  3.66 us
    ppermute x1, starting transfers between devices, extended_2(): before = lax.ppermute(last, axis, up)  1.98 us
    mul x1, local copies, waits for them, and re-layouts, body(): jnp.transpose(taps_sum, (1, 0, 2)).reshape(own_rows, KW * in_width) * factor  1.95 us
  transfers between devices with their start and end apart: 4, of which 1 were waited for; matrix products, arithmetic and copies ran while one was open for 7% of the time, Pallas kernels for 0%

commit v1 on v0

--- a/solution.py
+++ b/solution.py
@@ -6,6 +6,22 @@
 
 KW = 3
 TAP_SPACING = 64
+
+
+def exchange_in_pairs(x, axis, split, join):
+    ways, here = (lax.axis_size(axis), lax.axis_index(axis))
+    width = x.shape[split] // ways
+    shape = list(x.shape)
+    shape[split] = width
+    height = shape[join]
+    shape[join] = height * ways
+    full = jnp.zeros(shape, x.dtype)
+    for mask in range(ways):
+        part = lax.dynamic_slice_in_dim(x, (here ^ mask) * width, width, axis=split)
+        if mask:
+            part = lax.ppermute(part, axis, [(d, d ^ mask) for d in range(ways)])
+        full = lax.dynamic_update_slice_in_dim(full, part, (here ^ mask) * height, axis=join)
+    return full
 
 
 def extended_2(x, sides, width):
@@ -51,7 +67,7 @@
     batch_count = lax.axis_size("batch")
     counted = batch_count * inputs.shape[0] * length * seq_count
     factor = 1.0 / math.sqrt(float(counted))
-    owned = lax.all_to_all(cotangent, "seq", split_axis=2, concat_axis=1, tiled=True)[0]
+    owned = exchange_in_pairs(cotangent, "seq", 2, 1)[0]
     own_rows = owned.shape[1]
     owned_padded = jnp.pad(owned, ((reach, reach), (0, 0)))
     whole_act = lax.all_gather(act[None], "seq", axis=1, tiled=True)[0]

time: 85.6 us -> 79.9 us (0.933)
  local copies, waits for them, and re-layouts: 5.77 us -> 4.11 us
  starting transfers between devices: 14 us -> 12.5 us
  blocking collectives: 10.3 us -> 8.83 us
  other arithmetic: 2.18 us -> 1.3 us
    all_to_all x1 -> x0, starting transfers between devices: 4.24 us -> none  [body(): lax.all_to_all(cotangent, 'seq', split_axis=2, concat_axis=1, tiled=True)[0]]
    ppermute x0 -> x3, starting transfers between devices: none -> 3.18 us  [exchange_in_pairs(): part = lax.ppermute(part, axis, [(d, d ^ mask) for d in range(ways)])]
    unnamed x11 -> x5, local copies, waits for them, and re-layouts: 3.66 us -> 0.88 us
    unnamed x1 -> x0, other arithmetic: 1.81 us -> none
    all_gather x1, blocking collectives: 10.3 us -> 8.83 us  [body(): whole_act = lax.all_gather(act[None], 'seq', axis=1, tiled=True)[0]]
    dynamic_slice x0 -> x1, local copies, waits for them, and re-layouts: none -> 1.15 us  [exchange_in_pairs(): part = lax.dynamic_slice_in_dim(x, (here ^ mask) * width, width, axis=split)]
    convert_element_type x1, other arithmetic: 0.09 us -> 1.02 us  [body(): act = activation.astype(jnp.bfloat16)]
  transfers between devices with their start and end apart: 4 -> 6, of which waited for: 1 -> 1; matrix products, arithmetic and copies ran while one was open for 7% -> 8% of each run, Pallas kernels for 0% -> 0%
where the time goes in v1:
time: 79.9 us; the launch traced here: 79.5 us
  waiting for transfers between devices  45.3 us (57%)
  starting transfers between devices  12.5 us (16%)
  blocking collectives  8.83 us (11%)
  matrix products  6.58 us (8%)
  local copies, waits for them, and re-layouts  4.11 us (5%)
  other arithmetic  1.3 us (2%)
  between operations  0.85 us (1%)
    all_to_all x1, waiting for transfers between devices, body(): lax.all_to_all(pieces, 'batch', split_axis=1, concat_axis=1, tiled=True)  45.3 us
    all_gather x1, blocking collectives, body(): whole_act = lax.all_gather(act[None], 'seq', axis=1, tiled=True)[0]  8.83 us
    all_to_all x1, starting transfers between devices, body(): lax.all_to_all(pieces, 'batch', split_axis=1, concat_axis=1, tiled=True)  5.9 us
    dot_general x3, matrix products, body(): jnp.dot(window, weight[:, tap_index * in_width:(tap_index + 1) * in_width...  5.55 us
    ppermute x3, starting transfers between devices, exchange_in_pairs(): part = lax.ppermute(part, axis, [(d, d ^ mask) for d in range(ways)])  3.18 us
    ppermute x1, starting transfers between devices, extended_2(): before = lax.ppermute(last, axis, up)  1.98 us
    mul x1, local copies, waits for them, and re-layouts, body(): jnp.transpose(taps_sum, (1, 0, 2)).reshape(own_rows, KW * in_width) * factor  1.92 us
  transfers between devices with their start and end apart: 6, of which 1 were waited for; matrix products, arithmetic and copies ran while one was open for 8% of the time, Pallas kernels for 0%

profile of v1, /device:TPU:0, one launch (start us, length us, event | category | flops | bytes accessed | tf_op | source)
XLA Modules:
  0.0 79.5 jit_solution(9160871531086692010)
XLA Ops:
  0.6 0.0 copy-start
  0.7 1.2 %constant_dynamic-slice_fusion = (bf16[1,128,192]{2,1,0:T(8,128)(2,1)S(1)}, bf16[1,128,192]{2,1,0:T(8,128)(2,1)S(1)}, bf16[1,128,192]{2,1,0:T(8,128)(2,1)S(1)}) fusion(bf16[1,128,768]{2,1,0:T(8,128)(2,1)} %param.4, s32[]{:T(128)S(6)} %select_n.30, s32[]{:T(128)S(6)} %select_n.26, s32[]{:T(128)S(6)} %select_n.28), kind=kLoop, calls=%fused_computation.48 | loop fusion | bytes 294924 | tf_op jit(solution)/shard_map/dynamic_slice | solution.py:20
  1.8 0.5 collective-permute-start.2
  2.3 2.6 %collective-permute-start.3 = (bf16[1,128,192]{2,1,0:T(8,128)(2,1)S(1)}, bf16[1,128,192]{2,1,0:T(8,128)(2,1)S(1)}, u32[]{:S(2)}, u32[]{:S(2)}) collective-permute-start(bf16[1,128,192]{2,1,0:T(8,128)(2,1)S(1)} %get-tuple-element.6), channel_id=1, source_target_pairs={{0,16},{8,24},{16,0},{24,8},{1,17},{9,25},{17,1},{25,9},{2,18},{10... | collective-permute-start | bytes 147464 | tf_op jit(solution)/shard_map/ppermute | solution.py:22
  4.9 0.1 collective-permute-start.4
  5.0 1.0 %fusion.30 = bf16[1,128,768]{2,1,0:T(8,128)(2,1)S(1)} fusion(bf16[1,128,768]{2,1,0:T(8,128)(2,1)} %param.3), kind=kLoop, calls=%fused_computation.34 | loop fusion | flops 589824 | bytes 393216 | tf_op jit(solution)/shard_map/convert_element_type | solution.py:55
  6.0 8.8 %all_gather.3 = bf16[1,512,768]{2,1,0:T(8,128)(2,1)S(1)} all-gather(bf16[1,128,768]{2,1,0:T(8,128)(2,1)S(1)} %fusion.30), channel_id=1, replica_groups=mesh['seq'=4,'batch'=8] {'seq'}, dimensions={1}, use_global_device_ids=true | all-gather | bytes 983040 | tf_op jit(solution)/shard_map/all_gather | solution.py:73
  14.9 0.0 copy-done
  14.9 0.1 bitcast_dynamic-update-slice_fusion.3
  15.0 0.0 collective-permute-done.2
  15.0 0.0 collective-permute-done.3
  15.1 0.0 collective-permute-done.4
  15.1 0.3 convolution_bitcast_fusion
  15.4 0.3 convolution_bitcast_fusion.1
  15.8 0.3 convolution_bitcast_fusion.2
  16.1 0.1 fusion
  16.3 1.9 %copy.6 = f32[192,3,768]{0,2,1:T(8,128)} copy(f32[192,3,768]{2,0,1:T(8,128)S(1)} %fusion) | data formatting | bytes 3538944 | tf_op jit(solution)/shard_map/mul | solution.py:85
  18.2 5.9 %all-to-all-start = ((f32[192,8,288]{0,2,1:T(8,128)}), f32[192,8,288]{0,2,1:T(8,128)S(1)}, u32[]{:S(2)}, u32[]{:S(2)}) async-start(f32[192,8,288]{0,2,1:T(8,128)} %bitcast.66), calls=%async_computation | async-start | bytes 4718592 | tf_op jit(solution)/shard_map/all_to_all | solution.py:87
  24.1 2.0 %collective-permute-start.1 = (bf16[1,64,768]{2,1,0:T(8,128)(2,1)S(1)}, bf16[1,64,768]{2,1,0:T(8,128)(2,1)S(1)}, u32[]{:S(2)}, u32[]{:S(2)}) collective-permute-start(bf16[1,64,768]{2,1,0:T(8,128)(2,1)S(1)} %get-tuple-element.8), channel_id=1, source_target_pairs={{0,8},{8,16},{16,24},{1,9},{9,17},{17,25},{2,10},{10,18},{18,26},{... | collective-permute-start | bytes 294920 | tf_op jit(solution)/shard_map/ppermute | solution.py:34
  26.1 0.0 copy-start.1
  26.1 1.4 %collective-permute-start = (bf16[1,64,768]{2,1,0:T(8,128)(2,1)S(1)}, bf16[1,64,768]{2,1,0:T(8,128)(2,1)S(1)}, u32[]{:S(2)}, u32[]{:S(2)}) collective-permute-start(bf16[1,64,768]{2,1,0:T(8,128)(2,1)S(1)} %get-tuple-element.7), channel_id=1, source_target_pairs={{8,0},{16,8},{24,16},{9,1},{17,9},{25,17},{10,2},{18,10},{26,18},{... | collective-permute-start | bytes 294920 | tf_op jit(solution)/shard_map/ppermute | solution.py:35
  27.5 1.6 %fusion.5 = f32[128,768]{1,0:T(8,128)S(1)} fusion(bf16[768,2304]{1,0:T(8,128)(2,1)} %param.5, bf16[1,128,768]{2,1,0:T(8,128)(2,1)S(1)} %copy-done), kind=kOutput, calls=%fused_computation.10 | convolution fusion | flops 150994944 | bytes 1769472 | tf_op jit(solution)/shard_map/dot_general | solution.py:60
  29.1 0.0 collective-permute-done.1
  29.2 1.6 %fusion.3 = f32[128,768]{1,0:T(8,128)S(1)} fusion(bf16[768,2304]{1,0:T(8,128)(2,1)} %param.5, bf16[1,128,768]{2,1,0:T(8,128)(2,1)S(1)} %copy-done, bf16[1,64,768]{2,1,0:T(8,128)(2,1)S(1)} %collective-permute-done.1), kind=kOutput, calls=%fused_computation.8 | convolution fusion | flops 151388160 | bytes 1867776 | tf_op jit(solution)/shard_map/dot_general | solution.py:60
  30.8 0.0 collective-permute-done
  30.8 0.0 copy-done.1
  30.8 2.4 %fusion.11 = bf16[1,128,768]{2,1,0:T(8,128)(2,1)} fusion(f32[128,768]{1,0:T(8,128)S(1)} %fusion.3, f32[128,768]{1,0:T(8,128)S(1)} %fusion.5, bf16[768,2304]{1,0:T(8,128)(2,1)} %param.5, bf16[1,128,768]{2,1,0:T(8,128)(2,1)S(1)} %copy-done.1, bf16[1,64,768]{2,1,0:T(8,128)(2,1)S(1)} %collective-permute-done, bf16[1,128,768]{2,1,0:T(8,128)(2,1)S(1)} %copy-done), kind=kOutput, calls=%fused_computation.14 | convolution fusion | flops 152666112 | bytes 2654208 | tf_op jit(solution)/shard_map/dot_general | solution.py:60
  33.1 45.3 %all-to-all-done = f32[192,8,288]{0,2,1:T(8,128)S(1)} async-done(((f32[192,8,288]{0,2,1:T(8,128)}), f32[192,8,288]{0,2,1:T(8,128)S(1)}, u32[]{:S(2)}, u32[]{:S(2)}) %all-to-all-start) | async-done | bytes 1769504 | tf_op jit(solution)/shard_map/all_to_all | solution.py:87
  78.5 0.2 reduce_sum.9
  78.6 0.9 %copy.7 = f32[192,288]{1,0:T(8,128)} copy(f32[192,288]{0,1:T(8,128)S(1)} %reduce_sum.9) | data formatting | bytes 442368
  (5 shorter events, 0.1 us)
Async XLA Ops:
  0.6 14.3 %copy-start = (bf16[1,128,768]{2,1,0:T(8,128)(2,1)S(1)}, bf16[1,128,768]{2,1,0:T(8,128)(2,1)}, u32[]{:S(2)}) copy-start(bf16[1,128,768]{2,1,0:T(8,128)(2,1)} %param.4) | copy-start | bytes 589828
  1.8 13.2 %collective-permute-start.2 = (bf16[1,128,192]{2,1,0:T(8,128)(2,1)S(1)}, bf16[1,128,192]{2,1,0:T(8,128)(2,1)S(1)}, u32[]{:S(2)}, u32[]{:S(2)}) collective-permute-start(bf16[1,128,192]{2,1,0:T(8,128)(2,1)S(1)} %get-tuple-element.5), channel_id=1, source_target_pairs={{0,8},{8,0},{16,24},{24,16},{1,9},{9,1},{17,25},{25,17},{2,10},{10... | collective-permute-start | bytes 147464 | tf_op jit(solution)/shard_map/ppermute | solution.py:22
  2.3 12.7 %collective-permute-start.3 = (bf16[1,128,192]{2,1,0:T(8,128)(2,1)S(1)}, bf16[1,128,192]{2,1,0:T(8,128)(2,1)S(1)}, u32[]{:S(2)}, u32[]{:S(2)}) collective-permute-start(bf16[1,128,192]{2,1,0:T(8,128)(2,1)S(1)} %get-tuple-element.6), channel_id=1, source_target_pairs={{0,16},{8,24},{16,0},{24,8},{1,17},{9,25},{17,1},{25,9},{2,18},{10... | collective-permute-start | bytes 147464 | tf_op jit(solution)/shard_map/ppermute | solution.py:22
  4.9 10.1 %collective-permute-start.4 = (bf16[1,128,192]{2,1,0:T(8,128)(2,1)S(1)}, bf16[1,128,192]{2,1,0:T(8,128)(2,1)S(1)}, u32[]{:S(2)}, u32[]{:S(2)}) collective-permute-start(bf16[1,128,192]{2,1,0:T(8,128)(2,1)S(1)} %get-tuple-element.4), channel_id=1, source_target_pairs={{0,24},{8,16},{16,8},{24,0},{1,25},{9,17},{17,9},{25,1},{2,26},{10... | collective-permute-start | bytes 147464 | tf_op jit(solution)/shard_map/ppermute | solution.py:22
  18.2 60.3 %all-to-all-start = ((f32[192,8,288]{0,2,1:T(8,128)}), f32[192,8,288]{0,2,1:T(8,128)S(1)}, u32[]{:S(2)}, u32[]{:S(2)}) async-start(f32[192,8,288]{0,2,1:T(8,128)} %bitcast.66), calls=%async_computation | async-start | bytes 4718592 | tf_op jit(solution)/shard_map/all_to_all | solution.py:87
  24.1 5.0 %collective-permute-start.1 = (bf16[1,64,768]{2,1,0:T(8,128)(2,1)S(1)}, bf16[1,64,768]{2,1,0:T(8,128)(2,1)S(1)}, u32[]{:S(2)}, u32[]{:S(2)}) collective-permute-start(bf16[1,64,768]{2,1,0:T(8,128)(2,1)S(1)} %get-tuple-element.8), channel_id=1, source_target_pairs={{0,8},{8,16},{16,24},{1,9},{9,17},{17,25},{2,10},{10,18},{18,26},{... | collective-permute-start | bytes 294920 | tf_op jit(solution)/shard_map/ppermute | solution.py:34
  26.1 4.7 %copy-start.1 = (bf16[1,128,768]{2,1,0:T(8,128)(2,1)S(1)}, bf16[1,128,768]{2,1,0:T(8,128)(2,1)}, u32[]{:S(2)}) copy-start(bf16[1,128,768]{2,1,0:T(8,128)(2,1)} %param.3) | copy-start | bytes 589828
  26.1 4.7 %collective-permute-start = (bf16[1,64,768]{2,1,0:T(8,128)(2,1)S(1)}, bf16[1,64,768]{2,1,0:T(8,128)(2,1)S(1)}, u32[]{:S(2)}, u32[]{:S(2)}) collective-permute-start(bf16[1,64,768]{2,1,0:T(8,128)(2,1)S(1)} %get-tuple-element.7), channel_id=1, source_target_pairs={{8,0},{16,8},{24,16},{9,1},{17,9},{25,17},{10,2},{18,10},{26,18},{... | collective-permute-start | bytes 294920 | tf_op jit(solution)/shard_map/ppermute | solution.py:35
